TPU v7x, 256 devices: a whole 4x4x8 slice. The times are simulated.
256 devices in a mesh: seq: 32 (over z, y_lo, core), mp: 8 (over y_hi, x).
Axes of the slice: x: 4, y: 4 (y_hi: 2, y_lo: 2; y = y_hi * 2 + y_lo), z: 8, core: 2. Of those that a mesh axis runs over, the one named last changes fastest.
Arguments:
- tokens: bfloat16 [12288, 3072], P('seq', 'mp'), may hold values from -6 to 6
- w_qkv: bfloat16 [3072, 3, 3072], P(None, None, 'mp'), may hold values from -1 to 1
- q_gain: float32 [128], replicated, may hold values from 0 to 5
- k_gain: float32 [128], replicated, may hold values from 0 to 5
- w_out: bfloat16 [3072, 3072], P('mp'), may hold values from -0.15625 to 0.15625
- neighbours: int32 [32, 6], replicated, may hold values from 0 to 31, as said below
- counts: int32 [32], replicated, may hold values from 1 to 6
Outputs:
- mixed: bfloat16 [12288, 3072], P('seq', 'mp')
Inputs may be any that keep to these rules, and one draw needn't show every extreme that they name: `neighbours`: each row lists distinct tiles, each within 4 tiles of the row's own tile counted cyclically modulo 32.
All inputs are finite; a program needn't handle non-finite values.
Results may differ from a plain program's by a relative error of at most 0.014.
Values may be sent and summed in bfloat16 or wider, within the bound.
No kernel may reach another device: no remote copies, remote signals or barrier semaphores. Data moves between devices by JAX's collectives and lax.ppermute only.
A program may use at most 128 MiB of HBM per device.

v0:
```python
import jax
import jax.numpy as jnp
from jax import lax
from jax.sharding import PartitionSpec as P

HD = 128
TILE = 384
REACH = 4
NB = 6


def passed_along(value, axis, steps):
    count = lax.axis_size(axis)
    pairs = [(source, (source + steps) % count) for source in range(count)]
    return lax.ppermute(value, axis, pairs)


def head_norm(projected, gain_vec):
    per_head = projected.reshape(projected.shape[0], -1, HD)
    factor = lax.rsqrt(jnp.mean(per_head * per_head, axis=-1, keepdims=True) + 1e-06)
    return (per_head * factor * gain_vec).astype(jnp.bfloat16)


def on_device(tokens, w_qkv, q_gain, k_gain, w_out, neighbours, counts):
    tok_rows = tokens.shape[0]
    columns = w_qkv.shape[2]
    heads_here = columns // HD
    tiles_here = tok_rows // TILE
    total_tiles = neighbours.shape[0]
    span_here = (REACH + tiles_here - 1) // tiles_here
    flat_w = w_qkv.reshape(w_qkv.shape[0], 3 * columns)
    projected = jnp.dot(
        lax.all_gather(tokens, "mp", axis=1, tiled=True), flat_w, preferred_element_type=jnp.float32
    )
    queries = head_norm(projected[:, :columns], q_gain)
    key_part = head_norm(projected[:, columns : 2 * columns], k_gain).reshape(tok_rows, columns)
    value_part = projected[:, 2 * columns :].astype(jnp.bfloat16)
    paired = jnp.stack([key_part, value_part])
    blocks = []
    for offset in range(-span_here, span_here + 1):
        if offset == 0:
            blocks.append(paired)
        else:
            blocks.append(passed_along(paired, "seq", -offset))
    window = jnp.concatenate(blocks, axis=1)
    window_tiles = (2 * span_here + 1) * tiles_here
    position = lax.axis_index("seq")
    first_tile = position * tiles_here - span_here * tiles_here
    listed = lax.dynamic_slice_in_dim(neighbours, position * tiles_here, tiles_here, 0)
    used_counts = lax.dynamic_slice_in_dim(counts, position * tiles_here, tiles_here, 0)
    relative = jnp.mod(listed - first_tile, total_tiles)
    slot_used = jnp.arange(NB, dtype=jnp.int32)[None, :] < used_counts[:, None]
    query_blocks = queries.reshape(tiles_here, TILE, heads_here, HD)
    factor = HD ** (-0.5)
    hits = (
        relative[:, :, None] == jnp.arange(window_tiles, dtype=jnp.int32)[None, None, :]
    ) & slot_used[:, :, None]
    tile_mask = jnp.any(hits, axis=1)
    key_mask = jnp.repeat(tile_mask, TILE, axis=1)
    near_keys = window[0].reshape(window_tiles * TILE, heads_here, HD)
    near_values = window[1].reshape(window_tiles * TILE, heads_here, HD)
    scores = (
        jnp.einsum("tqhd,khd->thqk", query_blocks, near_keys, preferred_element_type=jnp.float32)
        * factor
    )
    scores = jnp.where(key_mask[:, None, None, :], scores, -jnp.inf)
    highest = jnp.max(scores, axis=-1, keepdims=True)
    expo = jnp.exp(scores - highest)
    probs = (expo / jnp.sum(expo, axis=-1, keepdims=True)).astype(jnp.bfloat16)
    attended = jnp.einsum("thqk,khd->tqhd", probs, near_values, preferred_element_type=jnp.float32)
    attended = attended.astype(jnp.bfloat16).reshape(tok_rows, columns)
    mixed_t = lax.psum_scatter(
        lax.dot_general(
            w_out, attended, (((0,), (1,)), ((), ())), preferred_element_type=jnp.float32
        ).astype(jnp.bfloat16),
        "mp",
        scatter_dimension=0,
        tiled=True,
    ).astype(jnp.float32)
    return mixed_t.T.astype(jnp.bfloat16)


def solution(mesh):
    return jax.shard_map(
        on_device,
        mesh=mesh,
        in_specs=(P("seq", "mp"), P(None, None, "mp"), P(), P(), P("mp", None), P(), P()),
        out_specs=P("seq", "mp"),
        check_vma=False,
    )
```

profile of v0, /device:TPU:2, one launch (start us, length us, event | category | flops | bytes accessed | tf_op | source)
XLA Modules:
  0.0 287.8 jit_solution(6885400218139403413)
XLA Ops:
  7.3 10.3 %copy.31 = bf16[3072,3,384]{0,2,1:T(8,128)(2,1)} copy(bf16[3072,3,384]{2,0,1:T(8,128)(2,1)} %param.8) | data formatting | bytes 14155776 | tf_op args[1]
  17.6 59.3 %all-gather.2.cloned.1.call-done = bf16[384,3072]{1,0:T(8,128)(2,1)} async-done(((bf16[384,384]{1,0:T(8,128)(2,1)}), bf16[384,3072]{1,0:T(8,128)(2,1)}) %all-gather.2.cloned.1.call-update) | async-done | bytes 2359312 | tf_op jit(solution)/shard_map/all_gather | solution.py:33
  76.9 7.0 %fusion.21 = f32[384,1152]{1,0:T(8,128)S(1)} fusion(bf16[384,3072]{1,0:T(8,128)(2,1)} %all-gather.2.cloned.1.call-done, bf16[3072,1152]{0,1:T(8,128)(2,1)} %bitcast.63), kind=kOutput, calls=%fused_computation.47 | convolution fusion | flops 2717908992 | bytes 11206656 | tf_op jit(solution)/shard_map/dot_general | solution.py:32
  84.0 1.2 copy-done.2
  86.0 1.3 copy.32
  88.5 2.3 fusion.20
  91.7 1.6 collective-permute-start
  95.0 1.8 collective-permute-start.7
  96.9 1.3 collective-permute-start.3
  98.7 1.3 copy.36
  100.1 9.4 %collective-permute-done = bf16[2,384,384]{2,1,0:T(8,128)(2,1)} collective-permute-done((bf16[2,384,384]{2,1,0:T(8,128)(2,1)}, bf16[2,384,384]{2,1,0:T(8,128)(2,1)}, u32[]{:S(2)}, u32[]{:S(2)}) %collective-permute-start) | collective-permute-done | bytes 589856 | tf_op jit(solution)/shard_map/ppermute | solution.py:15
  109.6 1.1 constant_dynamic-update-slice_fusion.8
  110.7 3.0 %collective-permute-done.1 = bf16[2,384,384]{2,1,0:T(8,128)(2,1)} collective-permute-done((bf16[2,384,384]{2,1,0:T(8,128)(2,1)}, bf16[2,384,384]{2,1,0:T(8,128)(2,1)}, u32[]{:S(2)}, u32[]{:S(2)}) %collective-permute-start.1) | collective-permute-done | bytes 589856 | tf_op jit(solution)/shard_map/ppermute | solution.py:15
  113.7 8.1 %collective-permute-start.5 = (bf16[2,384,384]{2,1,0:T(8,128)(2,1)}, bf16[2,384,384]{2,1,0:T(8,128)(2,1)S(1)}, u32[]{:S(2)}, u32[]{:S(2)}) collective-permute-start(bf16[2,384,384]{2,1,0:T(8,128)(2,1)} %pad_maximum_fusion), channel_id=1, source_target_pairs={{0,240},{8,248},{16,0},{24,8},{32,16},{40,24},{48,32},{56,40},{64,... | collective-permute-start | bytes 1769480 | tf_op jit(solution)/shard_map/ppermute | solution.py:15
  121.8 1.2 constant_dynamic-update-slice_fusion.7
  123.0 14.8 %collective-permute-done.2 = bf16[2,384,384]{2,1,0:T(8,128)(2,1)} collective-permute-done((bf16[2,384,384]{2,1,0:T(8,128)(2,1)}, bf16[2,384,384]{2,1,0:T(8,128)(2,1)}, u32[]{:S(2)}, u32[]{:S(2)}) %collective-permute-start.2) | collective-permute-done | bytes 589856 | tf_op jit(solution)/shard_map/ppermute | solution.py:15
  137.8 4.2 %collective-permute-start.6 = (bf16[2,384,384]{2,1,0:T(8,128)(2,1)}, bf16[2,384,384]{2,1,0:T(8,128)(2,1)S(1)}, u32[]{:S(2)}, u32[]{:S(2)}) collective-permute-start(bf16[2,384,384]{2,1,0:T(8,128)(2,1)} %pad_maximum_fusion), channel_id=1, source_target_pairs={{0,232},{8,240},{16,248},{24,0},{32,8},{40,16},{48,24},{56,32},{64... | collective-permute-start | bytes 1769480 | tf_op jit(solution)/shard_map/ppermute | solution.py:15
  141.9 1.2 constant_dynamic-update-slice_fusion.6
  143.1 1.2 constant_dynamic-update-slice_fusion.5
  144.5 13.7 %collective-permute-done.5 = bf16[2,384,384]{2,1,0:T(8,128)(2,1)S(1)} collective-permute-done((bf16[2,384,384]{2,1,0:T(8,128)(2,1)}, bf16[2,384,384]{2,1,0:T(8,128)(2,1)S(1)}, u32[]{:S(2)}, u32[]{:S(2)}) %collective-permute-start.5) | collective-permute-done | bytes 589856 | tf_op jit(solution)/shard_map/ppermute | solution.py:15
  158.4 2.9 %collective-permute-done.6 = bf16[2,384,384]{2,1,0:T(8,128)(2,1)S(1)} collective-permute-done((bf16[2,384,384]{2,1,0:T(8,128)(2,1)}, bf16[2,384,384]{2,1,0:T(8,128)(2,1)S(1)}, u32[]{:S(2)}, u32[]{:S(2)}) %collective-permute-start.6) | collective-permute-done | bytes 589856 | tf_op jit(solution)/shard_map/ppermute | solution.py:15
  161.4 1.2 constant_dynamic-update-slice_fusion
  162.5 2.9 fusion.19
  165.4 4.5 %copy.35 = bf16[1,3456,384]{1,2,0:T(8,128)(2,1)} copy(bf16[1,3456,384]{2,1,0:T(8,128)(2,1)} %get-tuple-element.5) | data formatting | bytes 5308416 | tf_op jit(solution)/shard_map/slice | solution.py:60
  169.9 4.5 %copy.34 = bf16[1,3456,384]{1,2,0:T(8,128)(2,1)} copy(bf16[1,3456,384]{2,1,0:T(8,128)(2,1)} %get-tuple-element.6) | data formatting | bytes 5308416 | tf_op jit(solution)/shard_map/slice | solution.py:61
  174.5 5.7 %bitcast_reduce_fusion = (f32[3,384]{1,0:T(4,128)S(1)}, f32[3,3456,384]{2,1,0:T(8,128)S(1)}) fusion(pred[3456]{0:T(1024)(128)(4,1)S(1)} %broadcast_in_dim.13, bf16[3456,3,128]{0,2,1:T(8,128)(2,1)} %bitcast.62, f32[384,3,128]{0,2,1:T(8,128)S(1)} %bitcast.65, f32[128]{0:T(128)S(1)} %copy-done.3, f32[384,3]{0,1:T(4,128)S(1)} %add_rsqrt_fusion), kind=kOutput, calls=%fused_computation.1 | convolution fusion | flops 1031601024 | bytes 19182464 | tf_op jit(solution)/shard_map/tqhd,khd->thqk/dot_general | solution.py:63
  180.2 4.3 %fusion.1 = f32[3,384]{1,0:T(4,128)S(1)} fusion(f32[3,3456,384]{2,1,0:T(8,128)S(1)} %get-tuple-element.10, f32[3,384]{1,0:T(4,128)S(1)} %get-tuple-element.9, pred[3456]{0:T(1024)(128)(4,1)S(1)} %broadcast_in_dim.13), kind=kLoop, calls=%fused_computation.5 | loop fusion | flops 15924096 | bytes 15937920 | tf_op jit(solution)/shard_map/reduce_sum | solution.py:69
  184.5 4.7 %fusion.5 = bf16[3,128,384]{2,1,0:T(8,128)(2,1)S(1)} fusion(bf16[3456,3,128]{0,2,1:T(8,128)(2,1)S(1)} %bitcast.66, f32[3,384]{1,0:T(4,128)S(1)} %fusion.1, f32[3,384]{1,0:T(4,128)S(1)} %get-tuple-element.9, f32[3,3456,384]{2,1,0:T(8,128)S(1)} %get-tuple-element.10, pred[3456]{0:T(1024)(128)(4,1)S(1)} %broadcast_in_dim.13), kind=kOutput, calls=%fused_computation.10 | convolution fusion | flops 1039269888 | bytes 18887040 | tf_op jit(solution)/shard_map/thqk,khd->tqhd/dot_general | solution.py:70
  189.2 2.8 fusion.4
  192.1 4.3 %copy.43 = bf16[3072,384]{1,0:T(8,128)(2,1)} copy(bf16[3072,384]{0,1:T(8,128)(2,1)} %fusion.4) | data formatting | bytes 4718592
  196.4 82.7 %reduce-scatter.4.cloned.1.call-done = bf16[384,384]{1,0:T(8,128)(2,1)} async-done(((bf16[3072,384]{1,0:T(8,128)(2,1)}), bf16[384,384]{1,0:T(8,128)(2,1)}) %reduce-scatter.4.cloned.1.call-update) | async-done | bytes 294928
  279.1 1.8 copy.44
  (43 shorter events, 6.5 us)
Async XLA Ops:
  6.5 182.7 %copy-start = (bf16[384,3072]{1,0:T(8,128)(2,1)S(1)}, bf16[384,3072]{1,0:T(8,128)(2,1)}, u32[]{:S(2)}) copy-start(bf16[384,3072]{1,0:T(8,128)(2,1)} %param.11) | copy-start | bytes 7077892
  6.5 70.4 %all-gather.2.cloned.1.call-start = ((), (), s32[]{:S(2)}) async-start(), calls=%async_computation.1 | async-start | bytes 2654208 | tf_op jit(solution)/shard_map/all_gather | solution.py:33
  7.3 10.3 %copy-start.5 = (f32[128]{0:T(128)S(1)}, f32[128]{0:T(128)}, u32[]{:S(2)}) copy-start(f32[128]{0:T(128)} %param.10) | copy-start | bytes 1540
  7.3 271.8 %reduce-scatter.4.cloned.1.call-start = ((), (), s32[]{:S(2)}) async-start(), calls=%async_computation.2 | async-start | bytes 2654208
  83.9 1.2 copy-start.2
  83.9 9.4 %copy-start.6 = (s32[32]{0:T(128)S(1)}, s32[32]{0:T(128)}, u32[]{:S(2)}) copy-start(s32[32]{0:T(128)} %param.13) | copy-start | bytes 388
  83.9 10.0 %copy-start.4 = (s32[32,6]{0,1:T(8,128)S(1)}, s32[32,6]{0,1:T(8,128)}, u32[]{:S(2)}) copy-start(s32[32,6]{0,1:T(8,128)} %param.12) | copy-start | bytes 2308
  91.7 17.8 %collective-permute-start = (bf16[2,384,384]{2,1,0:T(8,128)(2,1)}, bf16[2,384,384]{2,1,0:T(8,128)(2,1)}, u32[]{:S(2)}, u32[]{:S(2)}) collective-permute-start(bf16[2,384,384]{2,1,0:T(8,128)(2,1)} %pad_maximum_fusion), channel_id=1, source_target_pairs={{0,32},{8,40},{16,48},{24,56},{32,64},{40,72},{48,80},{56,88},{64,... | collective-permute-start | bytes 1769480 | tf_op jit(solution)/shard_map/ppermute | solution.py:15
  94.7 18.9 %collective-permute-start.1 = (bf16[2,384,384]{2,1,0:T(8,128)(2,1)}, bf16[2,384,384]{2,1,0:T(8,128)(2,1)}, u32[]{:S(2)}, u32[]{:S(2)}) collective-permute-start(bf16[2,384,384]{2,1,0:T(8,128)(2,1)} %pad_maximum_fusion), channel_id=1, source_target_pairs={{0,24},{8,32},{16,40},{24,48},{32,56},{40,64},{48,72},{56,80},{64,... | collective-permute-start | bytes 1769480 | tf_op jit(solution)/shard_map/ppermute | solution.py:15
  95.0 66.3 %collective-permute-start.7 = (bf16[2,384,384]{2,1,0:T(8,128)(2,1)}, bf16[2,384,384]{2,1,0:T(8,128)(2,1)}, u32[]{:S(2)}, u32[]{:S(2)}) collective-permute-start(bf16[2,384,384]{2,1,0:T(8,128)(2,1)} %pad_maximum_fusion), channel_id=1, source_target_pairs={{0,224},{8,232},{16,240},{24,248},{32,0},{40,8},{48,16},{56,24},{6... | collective-permute-start | bytes 1769480 | tf_op jit(solution)/shard_map/ppermute | solution.py:15
  96.9 46.2 %collective-permute-start.3 = (bf16[2,384,384]{2,1,0:T(8,128)(2,1)}, bf16[2,384,384]{2,1,0:T(8,128)(2,1)}, u32[]{:S(2)}, u32[]{:S(2)}) collective-permute-start(bf16[2,384,384]{2,1,0:T(8,128)(2,1)} %pad_maximum_fusion), channel_id=1, source_target_pairs={{0,8},{8,16},{16,24},{24,32},{32,40},{40,48},{48,56},{56,64},{64,7... | collective-permute-start | bytes 1769480 | tf_op jit(solution)/shard_map/ppermute | solution.py:15
  98.2 39.6 %collective-permute-start.2 = (bf16[2,384,384]{2,1,0:T(8,128)(2,1)}, bf16[2,384,384]{2,1,0:T(8,128)(2,1)}, u32[]{:S(2)}, u32[]{:S(2)}) collective-permute-start(bf16[2,384,384]{2,1,0:T(8,128)(2,1)} %pad_maximum_fusion), channel_id=1, source_target_pairs={{0,16},{8,24},{16,32},{24,40},{32,48},{40,56},{48,64},{56,72},{64,... | collective-permute-start | bytes 1769480 | tf_op jit(solution)/shard_map/ppermute | solution.py:15
  109.5 34.8 %collective-permute-start.4 = (bf16[2,384,384]{2,1,0:T(8,128)(2,1)}, bf16[2,384,384]{2,1,0:T(8,128)(2,1)S(1)}, u32[]{:S(2)}, u32[]{:S(2)}) collective-permute-start(bf16[2,384,384]{2,1,0:T(8,128)(2,1)} %pad_maximum_fusion), channel_id=1, source_target_pairs={{0,248},{8,0},{16,8},{24,16},{32,24},{40,32},{48,40},{56,48},{64,5... | collective-permute-start | bytes 1769480 | tf_op jit(solution)/shard_map/ppermute | solution.py:15
  113.7 44.6 %collective-permute-start.5 = (bf16[2,384,384]{2,1,0:T(8,128)(2,1)}, bf16[2,384,384]{2,1,0:T(8,128)(2,1)S(1)}, u32[]{:S(2)}, u32[]{:S(2)}) collective-permute-start(bf16[2,384,384]{2,1,0:T(8,128)(2,1)} %pad_maximum_fusion), channel_id=1, source_target_pairs={{0,240},{8,248},{16,0},{24,8},{32,16},{40,24},{48,32},{56,40},{64,... | collective-permute-start | bytes 1769480 | tf_op jit(solution)/shard_map/ppermute | solution.py:15
  137.8 23.5 %collective-permute-start.6 = (bf16[2,384,384]{2,1,0:T(8,128)(2,1)}, bf16[2,384,384]{2,1,0:T(8,128)(2,1)S(1)}, u32[]{:S(2)}, u32[]{:S(2)}) collective-permute-start(bf16[2,384,384]{2,1,0:T(8,128)(2,1)} %pad_maximum_fusion), channel_id=1, source_target_pairs={{0,232},{8,240},{16,248},{24,0},{32,8},{40,16},{48,24},{56,32},{64... | collective-permute-start | bytes 1769480 | tf_op jit(solution)/shard_map/ppermute | solution.py:15
  165.4 9.1 %copy-start.3 = (f32[128]{0:T(128)S(1)}, f32[128]{0:T(128)}, u32[]{:S(2)}) copy-start(f32[128]{0:T(128)} %param.9) | copy-start | bytes 1540
  180.2 4.3 %copy-start.1 = (bf16[1,3456,384]{1,2,0:T(8,128)(2,1)S(1)}, bf16[1,3456,384]{1,2,0:T(8,128)(2,1)}, u32[]{:S(2)}) copy-start(bf16[1,3456,384]{1,2,0:T(8,128)(2,1)} %copy.34) | copy-start | bytes 7962628
Sparse Core Ops, SparseCore 0:
  9.8 67.0 all-gather.1
  196.5 82.5 reduce-scatter.3
where the time goes:
time: 289 us; the launch traced here: 288 us
  waiting for transfers between devices  187 us (65%)
  local copies, waits for them, and re-layouts  40 us (14%)
  matrix products  20.2 us (7%)
  starting transfers between devices  17.7 us (6%)
  between operations  13.6 us (5%)
  other arithmetic  9.58 us (3%)
    unnamed x3, waiting for transfers between devices  83.4 us
    all_gather x1, waiting for transfers between devices, on_device(): lax.all_gather(tokens, 'mp', axis=1, tiled=True)  59.3 us
    ppermute x8, waiting for transfers between devices, passed_along(): return lax.ppermute(value, axis, pairs)  43.9 us
    unnamed x24, local copies, waits for them, and re-layouts  22.5 us
    ppermute x8, starting transfers between devices, passed_along(): return lax.ppermute(value, axis, pairs)  17.7 us
    slice x2, local copies, waits for them, and re-layouts, on_device(): near_keys = window[0].reshape(window_tiles * TILE, heads_here, HD)  7.38 us
    dot_general x1, matrix products, on_device(): jnp.dot(lax.all_gather(tokens, 'mp', axis=1, tiled=True), flat_w, preferr...  6.96 us
  transfers between devices with their start and end apart: 10, of which 7 were waited for; matrix products, arithmetic and copies ran while one was open for 6% of the time, Pallas kernels for 0%

commit v1 on v0

--- a/solution.py
+++ b/solution.py
@@ -29,9 +29,11 @@
     total_tiles = neighbours.shape[0]
     span_here = (REACH + tiles_here - 1) // tiles_here
     flat_w = w_qkv.reshape(w_qkv.shape[0], 3 * columns)
-    projected = jnp.dot(
-        lax.all_gather(tokens, "mp", axis=1, tiled=True), flat_w, preferred_element_type=jnp.float32
+    compute_the_windows = lambda block_in: jnp.concatenate(
+        lax.all_to_all(jnp.stack([block_in for _ in range(lax.axis_size("mp"))]), "mp", 0, 0),
+        axis=1,
     )
+    projected = jnp.dot(compute_the_windows(tokens), flat_w, preferred_element_type=jnp.float32)
     queries = head_norm(projected[:, :columns], q_gain)
     key_part = head_norm(projected[:, columns : 2 * columns], k_gain).reshape(tok_rows, columns)
     value_part = projected[:, 2 * columns :].astype(jnp.bfloat16)

time: 289 us -> 264 us (0.913)
  waiting for transfers between devices: 187 us -> 148 us
  starting transfers between devices: 17.7 us -> 29.1 us
    all_gather x1 -> x0, waiting for transfers between devices: 59.3 us -> none  [on_device(): lax.all_gather(tokens, 'mp', axis=1, tiled=True)]
    all_to_all x0 -> x1, waiting for transfers between devices: none -> 19.9 us  [on_device(): lax.all_to_all(jnp.stack([block_in for _ in range(lax.axis_size('mp'))]),...]
    all_to_all x0 -> x1, starting transfers between devices: none -> 7.46 us  [on_device(): lax.all_to_all(jnp.stack([block_in for _ in range(lax.axis_size('mp'))]),...]
    ppermute x8, starting transfers between devices: 17.7 us -> 21.6 us  [passed_along(): return lax.ppermute(value, axis, pairs)]
    unnamed x3 -> x2, waiting for transfers between devices: 83.4 us -> 85.1 us
    unnamed x24 -> x25, local copies, waits for them, and re-layouts: 22.5 us -> 23.8 us
  transfers between devices with their start and end apart: 10 -> 10, of which waited for: 7 -> 7; matrix products, arithmetic and copies ran while one was open for 6% -> 7% of each run, Pallas kernels for 0% -> 0%
where the time goes in v1:
time: 264 us; the launch traced here: 263 us
  waiting for transfers between devices  148 us (56%)
  local copies, waits for them, and re-layouts  42.8 us (16%)
  starting transfers between devices  29.1 us (11%)
  matrix products  20.2 us (8%)
  between operations  13.6 us (5%)
  other arithmetic  9.56 us (4%)
    unnamed x2, waiting for transfers between devices  85.1 us
    ppermute x8, waiting for transfers between devices, passed_along(): return lax.ppermute(value, axis, pairs)  42.6 us
    unnamed x25, local copies, waits for them, and re-layouts  23.8 us
    ppermute x8, starting transfers between devices, passed_along(): return lax.ppermute(value, axis, pairs)  21.6 us
    all_to_all x1, waiting for transfers between devices, on_device(): lax.all_to_all(jnp.stack([block_in for _ in range(lax.axis_size('mp'))]),...  19.9 us
    all_to_all x1, starting transfers between devices, on_device(): lax.all_to_all(jnp.stack([block_in for _ in range(lax.axis_size('mp'))]),...  7.46 us
    slice x2, local copies, waits for them, and re-layouts, on_device(): near_keys = window[0].reshape(window_tiles * TILE, heads_here, HD)  7.36 us
    dot_general x1, matrix products, on_device(): jnp.dot(compute_the_windows(tokens), flat_w, preferred_element_type=jnp.f...  6.97 us
  transfers between devices with their start and end apart: 10, of which 7 were waited for; matrix products, arithmetic and copies ran while one was open for 7% of the time, Pallas kernels for 0%

profile of v1, /device:TPU:2, one launch (start us, length us, event | category | flops | bytes accessed | tf_op | source)
XLA Modules:
  0.0 262.8 jit_solution(15700486403941618136)
XLA Ops:
  6.5 1.3 copy.33
  7.9 1.6 stack.6
  9.5 7.5 %all-to-all-start = ((bf16[8,384,384]{1,2,0:T(8,128)(2,1)}), bf16[8,384,384]{1,2,0:T(8,128)(2,1)}, u32[]{:S(2)}, u32[]{:S(2)}) async-start(bf16[8,384,384]{1,2,0:T(8,128)(2,1)} %stack.6), calls=%async_computation | async-start | bytes 4718592 | tf_op jit(solution)/shard_map/all_to_all | solution.py:33
  16.9 10.3 %copy.34 = bf16[3072,3,384]{0,2,1:T(8,128)(2,1)} copy(bf16[3072,3,384]{2,0,1:T(8,128)(2,1)} %param.8) | data formatting | bytes 14155776 | tf_op args[1]
  27.2 19.9 %all-to-all-done = bf16[8,384,384]{1,2,0:T(8,128)(2,1)} async-done(((bf16[8,384,384]{1,2,0:T(8,128)(2,1)}), bf16[8,384,384]{1,2,0:T(8,128)(2,1)}, u32[]{:S(2)}, u32[]{:S(2)}) %all-to-all-start) | async-done | bytes 2359328 | tf_op jit(solution)/shard_map/all_to_all | solution.py:33
  47.1 7.0 %fusion.21 = f32[384,1152]{1,0:T(8,128)S(1)} fusion(bf16[384,3072]{0,1:T(8,128)(2,1)} %bitcast.1, bf16[3072,1152]{0,1:T(8,128)(2,1)} %bitcast.66), kind=kOutput, calls=%fused_computation.47 | convolution fusion | flops 2717908992 | bytes 11206656 | tf_op jit(solution)/shard_map/dot_general | solution.py:36
  56.2 1.3 copy.35
  58.7 2.4 fusion.20
  61.9 1.9 collective-permute-start
  65.5 4.0 %collective-permute-start.7 = (bf16[2,384,384]{2,1,0:T(8,128)(2,1)}, bf16[2,384,384]{2,1,0:T(8,128)(2,1)}, u32[]{:S(2)}, u32[]{:S(2)}) collective-permute-start(bf16[2,384,384]{2,1,0:T(8,128)(2,1)} %pad_maximum_fusion), channel_id=1, source_target_pairs={{0,224},{8,232},{16,240},{24,248},{32,0},{40,8},{48,16},{56,24},{6... | collective-permute-start | bytes 1769480 | tf_op jit(solution)/shard_map/ppermute | solution.py:15
  70.2 1.3 copy.39
  71.6 10.6 %collective-permute-done = bf16[2,384,384]{2,1,0:T(8,128)(2,1)} collective-permute-done((bf16[2,384,384]{2,1,0:T(8,128)(2,1)}, bf16[2,384,384]{2,1,0:T(8,128)(2,1)}, u32[]{:S(2)}, u32[]{:S(2)}) %collective-permute-start) | collective-permute-done | bytes 589856 | tf_op jit(solution)/shard_map/ppermute | solution.py:15
  83.4 3.2 %collective-permute-done.1 = bf16[2,384,384]{2,1,0:T(8,128)(2,1)} collective-permute-done((bf16[2,384,384]{2,1,0:T(8,128)(2,1)}, bf16[2,384,384]{2,1,0:T(8,128)(2,1)}, u32[]{:S(2)}, u32[]{:S(2)}) %collective-permute-start.1) | collective-permute-done | bytes 589856 | tf_op jit(solution)/shard_map/ppermute | solution.py:15
  86.6 8.0 %collective-permute-start.5 = (bf16[2,384,384]{2,1,0:T(8,128)(2,1)}, bf16[2,384,384]{2,1,0:T(8,128)(2,1)S(1)}, u32[]{:S(2)}, u32[]{:S(2)}) collective-permute-start(bf16[2,384,384]{2,1,0:T(8,128)(2,1)} %pad_maximum_fusion), channel_id=1, source_target_pairs={{0,240},{8,248},{16,0},{24,8},{32,16},{40,24},{48,32},{56,40},{64,... | collective-permute-start | bytes 1769480 | tf_op jit(solution)/shard_map/ppermute | solution.py:15
  94.6 1.2 constant_dynamic-update-slice_fusion.7
  95.8 12.0 %collective-permute-done.2 = bf16[2,384,384]{2,1,0:T(8,128)(2,1)} collective-permute-done((bf16[2,384,384]{2,1,0:T(8,128)(2,1)}, bf16[2,384,384]{2,1,0:T(8,128)(2,1)}, u32[]{:S(2)}, u32[]{:S(2)}) %collective-permute-start.2) | collective-permute-done | bytes 589856 | tf_op jit(solution)/shard_map/ppermute | solution.py:15
  107.7 6.9 %collective-permute-start.6 = (bf16[2,384,384]{2,1,0:T(8,128)(2,1)}, bf16[2,384,384]{2,1,0:T(8,128)(2,1)S(1)}, u32[]{:S(2)}, u32[]{:S(2)}) collective-permute-start(bf16[2,384,384]{2,1,0:T(8,128)(2,1)} %pad_maximum_fusion), channel_id=1, source_target_pairs={{0,232},{8,240},{16,248},{24,0},{32,8},{40,16},{48,24},{56,32},{64... | collective-permute-start | bytes 1769480 | tf_op jit(solution)/shard_map/ppermute | solution.py:15
  114.7 1.2 constant_dynamic-update-slice_fusion.6
  115.8 1.2 constant_dynamic-update-slice_fusion.5
  117.2 13.6 %collective-permute-done.5 = bf16[2,384,384]{2,1,0:T(8,128)(2,1)S(1)} collective-permute-done((bf16[2,384,384]{2,1,0:T(8,128)(2,1)}, bf16[2,384,384]{2,1,0:T(8,128)(2,1)S(1)}, u32[]{:S(2)}, u32[]{:S(2)}) %collective-permute-start.5) | collective-permute-done | bytes 589856 | tf_op jit(solution)/shard_map/ppermute | solution.py:15
  130.9 3.1 %collective-permute-done.6 = bf16[2,384,384]{2,1,0:T(8,128)(2,1)S(1)} collective-permute-done((bf16[2,384,384]{2,1,0:T(8,128)(2,1)}, bf16[2,384,384]{2,1,0:T(8,128)(2,1)S(1)}, u32[]{:S(2)}, u32[]{:S(2)}) %collective-permute-start.6) | collective-permute-done | bytes 589856 | tf_op jit(solution)/shard_map/ppermute | solution.py:15
  134.1 1.2 constant_dynamic-update-slice_fusion
  135.3 2.8 %fusion.19 = (bf16[1,3456,384]{2,1,0:T(8,128)(2,1)}, bf16[1,3456,384]{2,1,0:T(8,128)(2,1)}) fusion(bf16[2,3456,384]{2,1,0:T(8,128)(2,1)S(1)} %constant_dynamic-update-slice_fusion), kind=kLoop, calls=%fused_computation.45 | loop fusion | bytes 10616832 | tf_op jit(solution)/shard_map/slice | solution.py:62
  138.2 4.5 %copy.38 = bf16[1,3456,384]{1,2,0:T(8,128)(2,1)} copy(bf16[1,3456,384]{2,1,0:T(8,128)(2,1)} %get-tuple-element.5) | data formatting | bytes 5308416 | tf_op jit(solution)/shard_map/slice | solution.py:62
  142.7 4.5 %copy.37 = bf16[1,3456,384]{1,2,0:T(8,128)(2,1)} copy(bf16[1,3456,384]{2,1,0:T(8,128)(2,1)} %get-tuple-element.6) | data formatting | bytes 5308416 | tf_op jit(solution)/shard_map/slice | solution.py:63
  147.1 5.7 %bitcast_reduce_fusion = (f32[3,384]{1,0:T(4,128)S(1)}, f32[3,3456,384]{2,1,0:T(8,128)S(1)}) fusion(pred[3456]{0:T(1024)(128)(4,1)S(1)} %broadcast_in_dim.13, bf16[3456,3,128]{0,2,1:T(8,128)(2,1)} %bitcast.65, f32[384,3,128]{0,2,1:T(8,128)S(1)} %bitcast.68, f32[128]{0:T(128)S(1)} %copy-done.3, f32[384,3]{0,1:T(4,128)S(1)} %add_rsqrt_fusion), kind=kOutput, calls=%fused_computation.1 | convolution fusion | flops 1031601024 | bytes 19182464 | tf_op jit(solution)/shard_map/tqhd,khd->thqk/dot_general | solution.py:65
  152.9 4.3 %fusion.1 = f32[3,384]{1,0:T(4,128)S(1)} fusion(f32[3,3456,384]{2,1,0:T(8,128)S(1)} %get-tuple-element.10, f32[3,384]{1,0:T(4,128)S(1)} %get-tuple-element.9, pred[3456]{0:T(1024)(128)(4,1)S(1)} %broadcast_in_dim.13), kind=kLoop, calls=%fused_computation.5 | loop fusion | flops 15924096 | bytes 15937920 | tf_op jit(solution)/shard_map/reduce_sum | solution.py:71
  157.2 4.7 %fusion.5 = bf16[3,128,384]{2,1,0:T(8,128)(2,1)S(1)} fusion(bf16[3456,3,128]{0,2,1:T(8,128)(2,1)S(1)} %bitcast.69, f32[3,384]{1,0:T(4,128)S(1)} %fusion.1, f32[3,384]{1,0:T(4,128)S(1)} %get-tuple-element.9, f32[3,3456,384]{2,1,0:T(8,128)S(1)} %get-tuple-element.10, pred[3456]{0:T(1024)(128)(4,1)S(1)} %broadcast_in_dim.13), kind=kOutput, calls=%fused_computation.10 | convolution fusion | flops 1039269888 | bytes 18887040 | tf_op jit(solution)/shard_map/thqk,khd->tqhd/dot_general | solution.py:72
  161.9 2.8 %fusion.4 = bf16[3072,384]{0,1:T(8,128)(2,1)} fusion(bf16[384,384]{0,1:T(8,128)(2,1)S(1)} %bitcast.72, bf16[384,3072]{1,0:T(8,128)(2,1)S(1)} %copy-done), kind=kOutput, calls=%fused_computation.9 | convolution fusion | flops 907149312 | bytes 5013504 | tf_op jit(solution)/shard_map/dot_general | solution.py:75
  164.7 4.3 %copy.46 = bf16[3072,384]{1,0:T(8,128)(2,1)} copy(bf16[3072,384]{0,1:T(8,128)(2,1)} %fusion.4) | data formatting | bytes 4718592
  169.1 85.1 %reduce-scatter.4.cloned.1.call-done = bf16[384,384]{1,0:T(8,128)(2,1)} async-done(((bf16[3072,384]{1,0:T(8,128)(2,1)}), bf16[384,384]{1,0:T(8,128)(2,1)}) %reduce-scatter.4.cloned.1.call-update) | async-done | bytes 294928
  254.1 1.8 copy.47
  (44 shorter events, 8.1 us)
Async XLA Ops:
  6.5 155.4 %copy-start = (bf16[384,3072]{1,0:T(8,128)(2,1)S(1)}, bf16[384,3072]{1,0:T(8,128)(2,1)}, u32[]{:S(2)}) copy-start(bf16[384,3072]{1,0:T(8,128)(2,1)} %param.11) | copy-start | bytes 7077892
  9.5 37.6 %all-to-all-start = ((bf16[8,384,384]{1,2,0:T(8,128)(2,1)}), bf16[8,384,384]{1,2,0:T(8,128)(2,1)}, u32[]{:S(2)}, u32[]{:S(2)}) async-start(bf16[8,384,384]{1,2,0:T(8,128)(2,1)} %stack.6), calls=%async_computation | async-start | bytes 4718592 | tf_op jit(solution)/shard_map/all_to_all | solution.py:33
  16.9 10.3 %copy-start.5 = (f32[128]{0:T(128)S(1)}, f32[128]{0:T(128)}, u32[]{:S(2)}) copy-start(f32[128]{0:T(128)} %param.10) | copy-start | bytes 1540
  16.9 237.2 %reduce-scatter.4.cloned.1.call-start = ((), (), s32[]{:S(2)}) async-start(), calls=%async_computation.2 | async-start | bytes 2654208
  54.1 1.2 copy-start.2
  54.1 9.7 %copy-start.6 = (s32[32]{0:T(128)S(1)}, s32[32]{0:T(128)}, u32[]{:S(2)}) copy-start(s32[32]{0:T(128)} %param.13) | copy-start | bytes 388
  54.1 10.3 %copy-start.4 = (s32[32,6]{0,1:T(8,128)S(1)}, s32[32,6]{0,1:T(8,128)}, u32[]{:S(2)}) copy-start(s32[32,6]{0,1:T(8,128)} %param.12) | copy-start | bytes 2308
  61.9 20.3 %collective-permute-start = (bf16[2,384,384]{2,1,0:T(8,128)(2,1)}, bf16[2,384,384]{2,1,0:T(8,128)(2,1)}, u32[]{:S(2)}, u32[]{:S(2)}) collective-permute-start(bf16[2,384,384]{2,1,0:T(8,128)(2,1)} %pad_maximum_fusion), channel_id=1, source_target_pairs={{0,32},{8,40},{16,48},{24,56},{32,64},{40,72},{48,80},{56,88},{64,... | collective-permute-start | bytes 1769480 | tf_op jit(solution)/shard_map/ppermute | solution.py:15
  65.3 21.3 %collective-permute-start.1 = (bf16[2,384,384]{2,1,0:T(8,128)(2,1)}, bf16[2,384,384]{2,1,0:T(8,128)(2,1)}, u32[]{:S(2)}, u32[]{:S(2)}) collective-permute-start(bf16[2,384,384]{2,1,0:T(8,128)(2,1)} %pad_maximum_fusion), channel_id=1, source_target_pairs={{0,24},{8,32},{16,40},{24,48},{32,56},{40,64},{48,72},{56,80},{64,... | collective-permute-start | bytes 1769480 | tf_op jit(solution)/shard_map/ppermute | solution.py:15
  65.5 68.6 %collective-permute-start.7 = (bf16[2,384,384]{2,1,0:T(8,128)(2,1)}, bf16[2,384,384]{2,1,0:T(8,128)(2,1)}, u32[]{:S(2)}, u32[]{:S(2)}) collective-permute-start(bf16[2,384,384]{2,1,0:T(8,128)(2,1)} %pad_maximum_fusion), channel_id=1, source_target_pairs={{0,224},{8,232},{16,240},{24,248},{32,0},{40,8},{48,16},{56,24},{6... | collective-permute-start | bytes 1769480 | tf_op jit(solution)/shard_map/ppermute | solution.py:15
  69.6 46.2 %collective-permute-start.3 = (bf16[2,384,384]{2,1,0:T(8,128)(2,1)}, bf16[2,384,384]{2,1,0:T(8,128)(2,1)}, u32[]{:S(2)}, u32[]{:S(2)}) collective-permute-start(bf16[2,384,384]{2,1,0:T(8,128)(2,1)} %pad_maximum_fusion), channel_id=1, source_target_pairs={{0,8},{8,16},{16,24},{24,32},{32,40},{40,48},{48,56},{56,64},{64,7... | collective-permute-start | bytes 1769480 | tf_op jit(solution)/shard_map/ppermute | solution.py:15
  69.6 38.2 %collective-permute-start.2 = (bf16[2,384,384]{2,1,0:T(8,128)(2,1)}, bf16[2,384,384]{2,1,0:T(8,128)(2,1)}, u32[]{:S(2)}, u32[]{:S(2)}) collective-permute-start(bf16[2,384,384]{2,1,0:T(8,128)(2,1)} %pad_maximum_fusion), channel_id=1, source_target_pairs={{0,16},{8,24},{16,32},{24,40},{32,48},{40,56},{48,64},{56,72},{64,... | collective-permute-start | bytes 1769480 | tf_op jit(solution)/shard_map/ppermute | solution.py:15
  82.3 34.8 %collective-permute-start.4 = (bf16[2,384,384]{2,1,0:T(8,128)(2,1)}, bf16[2,384,384]{2,1,0:T(8,128)(2,1)S(1)}, u32[]{:S(2)}, u32[]{:S(2)}) collective-permute-start(bf16[2,384,384]{2,1,0:T(8,128)(2,1)} %pad_maximum_fusion), channel_id=1, source_target_pairs={{0,248},{8,0},{16,8},{24,16},{32,24},{40,32},{48,40},{56,48},{64,5... | collective-permute-start | bytes 1769480 | tf_op jit(solution)/shard_map/ppermute | solution.py:15
  86.6 44.2 %collective-permute-start.5 = (bf16[2,384,384]{2,1,0:T(8,128)(2,1)}, bf16[2,384,384]{2,1,0:T(8,128)(2,1)S(1)}, u32[]{:S(2)}, u32[]{:S(2)}) collective-permute-start(bf16[2,384,384]{2,1,0:T(8,128)(2,1)} %pad_maximum_fusion), channel_id=1, source_target_pairs={{0,240},{8,248},{16,0},{24,8},{32,16},{40,24},{48,32},{56,40},{64,... | collective-permute-start | bytes 1769480 | tf_op jit(solution)/shard_map/ppermute | solution.py:15
  107.7 26.3 %collective-permute-start.6 = (bf16[2,384,384]{2,1,0:T(8,128)(2,1)}, bf16[2,384,384]{2,1,0:T(8,128)(2,1)S(1)}, u32[]{:S(2)}, u32[]{:S(2)}) collective-permute-start(bf16[2,384,384]{2,1,0:T(8,128)(2,1)} %pad_maximum_fusion), channel_id=1, source_target_pairs={{0,232},{8,240},{16,248},{24,0},{32,8},{40,16},{48,24},{56,32},{64... | collective-permute-start | bytes 1769480 | tf_op jit(solution)/shard_map/ppermute | solution.py:15
  138.2 9.0 %copy-start.3 = (f32[128]{0:T(128)S(1)}, f32[128]{0:T(128)}, u32[]{:S(2)}) copy-start(f32[128]{0:T(128)} %param.9) | copy-start | bytes 1540
  152.9 4.3 %copy-start.1 = (bf16[1,3456,384]{1,2,0:T(8,128)(2,1)S(1)}, bf16[1,3456,384]{1,2,0:T(8,128)(2,1)}, u32[]{:S(2)}) copy-start(bf16[1,3456,384]{1,2,0:T(8,128)(2,1)} %copy.37) | copy-start | bytes 7962628
Sparse Core Ops, SparseCore 0:
  169.2 84.8 reduce-scatter.3
